TPU v7x, 32 devices: a whole 2x2x4 slice. The times are simulated.
32 devices in a mesh: pipe: 4 (over z), sx: 4 (over y, x), sy: 2 (over core).
Axes of the slice: x: 2, y: 2, z: 4, core: 2. Of those that a mesh axis runs over, the one named last changes fastest.
Arguments:
- segment_inputs: bfloat16 [4, 1, 4, 2, 512, 128], P('pipe', None, 'sx', 'sy'), may hold values from -6 to 6
- out_cotangent: bfloat16 [1, 4, 2, 512, 128], P(None, 'sx', 'sy'), may hold values from -6 to 6
- neighbours: int32 [1, 4, 2, 1, 27], P(None, 'sx', 'sy'), may hold values from 0 to 1, as said below
- block_counts: int32 [1, 4, 2], P(None, 'sx', 'sy'), may hold values from 1 to 1, as said below
- norm_gain: float32 [4, 128], P('pipe'), may hold values from 0.1 to 1.9
- kernel: bfloat16 [4, 3456, 128], P('pipe', 'sx'), may hold values from -0.109375 to 0.109375
Outputs:
- grad_inputs: bfloat16 [4, 1, 4, 2, 512, 128], P('pipe', None, 'sx', 'sy')
- kernel_grad: float32 [4, 3456, 128], P('pipe', 'sx')
Inputs may be any that keep to these rules, and one draw needn't show every extreme that they name: `neighbours`: entry [m, a, b, s, (i + 1) * 9 + (j + 1) * 3 + (k + 1)], i, j, k in -1..1, is the slot in the list of slab (a + i, b + j) of the occupied block lying i, j, k blocks from slot s of slab (a, b) along x, y, z, or 1 where that block is not occupied, the slab is off the grid, or slot s is padding; it never names a padding slot. `block_counts`: slots 0 to count - 1 of a slab's list hold its occupied blocks; later slots are padding.
All inputs are finite; a program needn't handle non-finite values.
Results may differ from a plain program's by a relative error of at most 0.014.
Values may be sent and summed in bfloat16 or wider, within the bound.
No kernel may reach another device: no remote copies, remote signals or barrier semaphores. Data moves between devices by JAX's collectives and lax.ppermute only.
A program may use at most 64 MiB of HBM per device.

v0:
```python
import jax
import jax.numpy as jnp
from jax import lax
from jax.sharding import PartitionSpec as P

OFFSETS = (-1, 0, 1)


def source_range(offset):
    if offset < 0:
        return slice(7, 8)
    if offset > 0:
        return slice(0, 1)
    return slice(0, 8)


def activate(values, gain_row):
    floats = values.astype(jnp.float32)
    square = jnp.mean(floats * floats, axis=-1, keepdims=True)
    return jax.nn.silu(floats * lax.rsqrt(square + 1e-06) * gain_row)


def with_blank(blocks_in):
    return jnp.concatenate([blocks_in, jnp.zeros_like(blocks_in)], axis=0)


def face_piece(cube, shift_x, shift_y):
    return cube[:, source_range(shift_x), source_range(shift_y)]


def directions():
    return [(sx, sy) for sx in OFFSETS for sy in OFFSETS if (sx, sy) != (0, 0)]


def assemble(centre, received, table):
    slabs_x = []
    for shift_x in OFFSETS:
        rows_y = []
        for shift_y in OFFSETS:
            column = (shift_x + 1) * 3 + (shift_y + 1)
            source = with_blank(
                centre if (shift_x, shift_y) == (0, 0) else received[shift_x, shift_y]
            )
            parts_z = []
            for shift_z in OFFSETS:
                direction = column * 3 + shift_z + 1
                picked = source[table[:, direction]]
                parts_z.append(picked[:, :, :, source_range(shift_z), :])
            rows_y.append(jnp.concatenate(parts_z, axis=3))
        slabs_x.append(jnp.concatenate(rows_y, axis=2))
    return jnp.concatenate(slabs_x, axis=1)


def exchange(cube, axes, sizes, pipe_step):
    received = {}
    for shift_x, shift_y in directions():
        piece = face_piece(cube, shift_x, shift_y)
        route = []
        if pipe_step:
            n_pipe, n_x, n_y = sizes
            for p in range(pipe_step, n_pipe):
                for a in range(n_x):
                    for b in range(n_y):
                        ta, tb = (a - shift_x, b - shift_y)
                        if 0 <= ta < n_x and 0 <= tb < n_y:
                            route.append(
                                ((p * n_x + a) * n_y + b, ((p - pipe_step) * n_x + ta) * n_y + tb)
                            )
        else:
            n_x, n_y = sizes
            for a in range(n_x):
                for b in range(n_y):
                    ta, tb = (a - shift_x, b - shift_y)
                    if 0 <= ta < n_x and 0 <= tb < n_y:
                        route.append((a * n_y + b, ta * n_y + tb))
        received[shift_x, shift_y] = lax.ppermute(piece, axes, route)
    return received


def columns(padded, rows, sign):
    taps = []
    for tap_x in OFFSETS:
        for tap_y in OFFSETS:
            for tap_z in OFFSETS:
                taps.append(
                    padded[
                        :,
                        1 + sign * tap_x : 9 + sign * tap_x,
                        1 + sign * tap_y : 9 + sign * tap_y,
                        1 + sign * tap_z : 9 + sign * tap_z,
                        :,
                    ]
                )
    stacked = jnp.stack(taps, axis=-2)
    return stacked.reshape(rows, len(taps) * padded.shape[-1])


def finish_grad(values, grad_live, live_now, grad_act, gain_row):
    _, pullback = jax.vjp(lambda floats: activate(floats, gain_row), values.astype(jnp.float32))
    (through,) = pullback(grad_act)
    summed = grad_live.astype(jnp.float32) + through
    result = jnp.where(live_now[:, None], summed, jnp.zeros_like(summed))
    return result.astype(jnp.bfloat16)


def shards(segment_inputs, out_cotangent, neighbours, block_counts, norm_gain, kernel):
    n_pipe = lax.axis_size("pipe")
    n_x = lax.axis_size("sx")
    n_y = lax.axis_size("sy")
    segment_place = lax.axis_index("pipe")
    micro_count = segment_inputs.shape[1]
    row_count = segment_inputs.shape[4]
    channels = segment_inputs.shape[5]
    blocks = row_count // 512
    taps = 27
    weights = lax.all_gather(kernel[0], "sx", axis=0, tiled=True)
    flipped = (
        weights.reshape(taps, channels, channels)
        .transpose(0, 2, 1)
        .reshape(taps * channels, channels)
    )
    gain_row = norm_gain[0]
    inputs = segment_inputs[0, :, 0, 0]
    cotangent = out_cotangent[:, 0, 0]
    tables = neighbours[:, 0, 0]
    slot_ids = jnp.arange(row_count, dtype=jnp.int32) // 512
    live_rows = slot_ids[None, :] < block_counts[:, 0, 0][:, None]

    def cube(values):
        return values.reshape(blocks, 8, 8, 8, channels)

    grads_out = []
    kernel_total = jnp.zeros((taps * channels, channels), jnp.float32)
    for micro in range(micro_count):
        table = tables[micro]
        live_now = live_rows[micro]
        values = inputs[micro]
        activation = activate(values, gain_row).astype(jnp.bfloat16)
        start = cotangent[micro]
        start = jnp.where(live_now[:, None], start, jnp.zeros_like(start))
        both = jnp.concatenate([cube(activation), cube(start)], axis=-1)
        got = exchange(both, ("sx", "sy"), (n_x, n_y), 0)
        act_pad = assemble(cube(activation), {k: v[..., :channels] for k, v in got.items()}, table)
        act_cols = columns(act_pad, row_count, 1)
        centre = start
        received = {k: v[..., channels:] for k, v in got.items()}
        kept_dy = start
        kept_grad = jnp.zeros((row_count, channels), jnp.bfloat16)
        for tick in range(n_pipe):
            active = segment_place == n_pipe - 1 - tick
            grad_pad = assemble(cube(centre), received, table)
            grad_act = jnp.dot(
                columns(grad_pad, row_count, -1), flipped, preferred_element_type=jnp.float32
            )
            result = finish_grad(values, centre, live_now, grad_act, gain_row)
            kept_dy = jnp.where(active, centre, kept_dy)
            kept_grad = jnp.where(active, result, kept_grad)
            if tick < n_pipe - 1:
                down = [(p, p - 1) for p in range(1, n_pipe)]
                centre = lax.ppermute(result, "pipe", down)
                received = exchange(cube(result), ("pipe", "sx", "sy"), (n_pipe, n_x, n_y), 1)
        kernel_total = kernel_total + lax.dot_general(
            act_cols, kept_dy, (((0,), (0,)), ((), ())), preferred_element_type=jnp.float32
        )
        grads_out.append(kept_grad)
    grad_store = jnp.stack(grads_out)
    norm_scale = float(n_x * n_y * micro_count * row_count) ** (-0.5)
    kernel_term = kernel_total * norm_scale
    shard_rows = kernel.shape[1]
    summed = lax.psum(kernel_term.astype(jnp.bfloat16), "sy").astype(jnp.float32)
    kernel_share = lax.psum_scatter(
        lax.slice_in_dim(summed, 0, shard_rows * n_x, axis=0).astype(jnp.bfloat16),
        "sx",
        scatter_dimension=0,
        tiled=True,
    ).astype(jnp.float32)
    return (grad_store[None, :, None, None], kernel_share[None])


def solution(mesh):
    return jax.shard_map(
        shards,
        mesh=mesh,
        in_specs=(
            P("pipe", None, "sx", "sy", None, None),
            P(None, "sx", "sy", None, None),
            P(None, "sx", "sy", None, None),
            P(None, "sx", "sy"),
            P("pipe", None),
            P("pipe", "sx", None),
        ),
        out_specs=(P("pipe", None, "sx", "sy", None, None), P("pipe", "sx", None)),
        check_vma=False,
    )
```

profile of v0, /device:TPU:0, one launch (start us, length us, event | category | flops | bytes accessed | tf_op | source)
XLA Modules:
  0.0 277.4 jit_solution(7714859741776979580)
XLA Ops:
  11.2 1.3 collective-permute-start.4
  12.5 4.8 %collective-permute-start.6 = (bf16[1,1,8,8,256]{4,3,2,1,0:T(8,128)(2,1)S(1)}, bf16[1,1,8,8,256]{4,3,2,1,0:T(8,128)(2,1)S(1)}, u32[]{:S(2)}, u32[]{:S(2)}) collective-permute-start(bf16[1,1,8,8,256]{4,3,2,1,0:T(8,128)(2,1)S(1)} %get-tuple-element.1491), channel_id=1, source_target_pairs={{0,2},{1,3},{2,4},{3,5},{4,6},{5,7},{8,10},{9,11},{10,12},{11,13},... | collective-permute-start | bytes 98312 | tf_op jit(solution)/shard_map/ppermute | solution.py:76
  17.4 1.3 collective-permute-start.3
  19.4 1.3 collective-permute-start.1
  20.7 2.1 fusion.89
  36.6 1.6 fusion.90
  46.1 19.6 %all-gather = bf16[1,3456,128]{2,1,0:T(8,128)(2,1)S(1)} all-gather(bf16[1,864,128]{2,1,0:T(8,128)(2,1)} %param.11), channel_id=2, replica_groups=mesh['pipe'=4,'sx'=4,'sy'=2] {'sx'}, dimensions={1}, use_global_device_ids=true | all-gather | bytes 1105920 | tf_op jit(solution)/shard_map/all_gather | solution.py:116
  80.3 1.3 copy.138
  96.8 1.6 collective-permute-start
  99.2 6.2 %collective-permute-start.5 = (bf16[1,1,1,8,256]{4,3,2,1,0:T(8,128)(2,1)S(1)}, bf16[1,1,1,8,256]{4,3,2,1,0:T(8,128)(2,1)S(1)}, u32[]{:S(2)}, u32[]{:S(2)}) collective-permute-start(bf16[1,1,1,8,256]{4,3,2,1,0:T(8,128)(2,1)S(1)} %get-tuple-element.1487), channel_id=1, source_target_pairs={{0,3},{2,5},{4,7},{8,11},{10,13},{12,15},{16,19},{18,21},{20,23},{... | collective-permute-start | bytes 12296 | tf_op jit(solution)/shard_map/ppermute | solution.py:76
  105.4 1.3 collective-permute-done.5
  110.0 1.2 fusion.35
  111.5 1.3 collective-permute-start.8
  113.0 1.3 collective-permute-start.13
  114.3 1.3 collective-permute-start.12
  116.3 1.3 collective-permute-start.10
  126.9 1.2 fusion.36
  128.5 1.3 collective-permute-start.17
  129.8 1.3 collective-permute-start.22
  131.1 1.3 collective-permute-start.21
  133.1 1.3 collective-permute-start.19
  134.4 15.8 %collective-permute-done.22 = bf16[1,1,1,8,128]{4,3,2,1,0:T(8,128)(2,1)S(1)} collective-permute-done((bf16[1,1,1,8,128]{4,3,2,1,0:T(8,128)(2,1)S(1)}, bf16[1,1,1,8,128]{4,3,2,1,0:T(8,128)(2,1)S(1)}, u32[]{:S(2)}, u32[]{:S(2)}) %collective-permute-start.22) | collective-permute-done | bytes 2080 | tf_op jit(solution)/shard_map/ppermute | solution.py:76
  157.7 1.3 collective-permute-start.26
  159.1 1.3 collective-permute-start.31
  160.4 1.3 collective-permute-start.30
  162.4 1.3 collective-permute-start.28
  163.7 19.4 %collective-permute-done.31 = bf16[1,1,1,8,128]{4,3,2,1,0:T(8,128)(2,1)S(1)} collective-permute-done((bf16[1,1,1,8,128]{4,3,2,1,0:T(8,128)(2,1)S(1)}, bf16[1,1,1,8,128]{4,3,2,1,0:T(8,128)(2,1)S(1)}, u32[]{:S(2)}, u32[]{:S(2)}) %collective-permute-start.31) | collective-permute-done | bytes 2080 | tf_op jit(solution)/shard_map/ppermute | solution.py:76
  202.5 2.2 fusion
  209.1 3.2 %fusion.38 = (f32[512]{0:T(512)S(1)}, f32[512,128]{1,0:T(8,128)S(1)}) fusion(bf16[1,1,1,1,512,128]{5,4,3,2,1,0:T(8,128)(2,1)S(1)} %copy-done, f32[128]{0:T(128)S(1)} %bitcast.970, f32[512]{0:T(512)S(1)} %fusion.70, bf16[512,3456]{1,0:T(8,128)(2,1)} %bitcast.281, bf16[3456,128]{1,0:T(8,128)(2,1)S(1)} %bitcast.950), kind=kOutput, calls=%fused_computation.238 | convolution fusion | flops 453967360 | bytes 4821504 | tf_op jit(solution)/shard_map/dot_general | solution.py:152
  212.3 36.1 %reduce-scatter.2.cloned.1.call-done = bf16[864,128]{1,0:T(8,128)(2,1)} async-done(((bf16[3456,128]{1,0:T(8,128)(2,1)}), bf16[864,128]{1,0:T(8,128)(2,1)}) %reduce-scatter.2.cloned.1.call-update) | async-done | bytes 221200 | tf_op jit(solution)/shard_map/reduce_scatter | solution.py:171
  249.4 19.4 %all-reduce.47.cloned.1.call-done = bf16[864,128]{1,0:T(8,128)(2,1)} async-done(((bf16[864,128]{1,0:T(8,128)(2,1)}), bf16[864,128]{1,0:T(8,128)(2,1)}) %all-reduce.47.cloned.1.call-update) | async-done | bytes 221200 | tf_op jit(solution)/shard_map/psum | solution.py:170
  268.8 1.7 bitcast_convert_fusion
  (346 shorter events, 51.4 us)
Async XLA Ops:
  7.2 241.2 %reduce-scatter.2.cloned.1.call-start = ((), (), s32[]{:S(2)}) async-start(), calls=%async_computation.1 | async-start | bytes 1105920 | tf_op jit(solution)/shard_map/reduce_scatter | solution.py:171
  11.2 85.6 %collective-permute-start.4 = (bf16[1,1,1,8,256]{4,3,2,1,0:T(8,128)(2,1)S(1)}, bf16[1,1,1,8,256]{4,3,2,1,0:T(8,128)(2,1)S(1)}, u32[]{:S(2)}, u32[]{:S(2)}) collective-permute-start(bf16[1,1,1,8,256]{4,3,2,1,0:T(8,128)(2,1)S(1)} %get-tuple-element.1489), channel_id=1, source_target_pairs={{3,0},{5,2},{7,4},{11,8},{13,10},{15,12},{19,16},{21,18},{23,20},{... | collective-permute-start | bytes 12296 | tf_op jit(solution)/shard_map/ppermute | solution.py:76
  12.5 94.6 %collective-permute-start.6 = (bf16[1,1,8,8,256]{4,3,2,1,0:T(8,128)(2,1)S(1)}, bf16[1,1,8,8,256]{4,3,2,1,0:T(8,128)(2,1)S(1)}, u32[]{:S(2)}, u32[]{:S(2)}) collective-permute-start(bf16[1,1,8,8,256]{4,3,2,1,0:T(8,128)(2,1)S(1)} %get-tuple-element.1491), channel_id=1, source_target_pairs={{0,2},{1,3},{2,4},{3,5},{4,6},{5,7},{8,10},{9,11},{10,12},{11,13},... | collective-permute-start | bytes 98312 | tf_op jit(solution)/shard_map/ppermute | solution.py:76
  17.4 89.5 %collective-permute-start.3 = (bf16[1,1,8,8,256]{4,3,2,1,0:T(8,128)(2,1)S(1)}, bf16[1,1,8,8,256]{4,3,2,1,0:T(8,128)(2,1)S(1)}, u32[]{:S(2)}, u32[]{:S(2)}) collective-permute-start(bf16[1,1,8,8,256]{4,3,2,1,0:T(8,128)(2,1)S(1)} %get-tuple-element.1492), channel_id=1, source_target_pairs={{2,0},{3,1},{4,2},{5,3},{6,4},{7,5},{10,8},{11,9},{12,10},{13,11},... | collective-permute-start | bytes 98312 | tf_op jit(solution)/shard_map/ppermute | solution.py:76
  18.7 79.8 %collective-permute-start.2 = (bf16[1,1,1,8,256]{4,3,2,1,0:T(8,128)(2,1)S(1)}, bf16[1,1,1,8,256]{4,3,2,1,0:T(8,128)(2,1)S(1)}, u32[]{:S(2)}, u32[]{:S(2)}) collective-permute-start(bf16[1,1,1,8,256]{4,3,2,1,0:T(8,128)(2,1)S(1)} %get-tuple-element.1488), channel_id=1, source_target_pairs={{2,1},{4,3},{6,5},{10,9},{12,11},{14,13},{18,17},{20,19},{22,21},{... | collective-permute-start | bytes 12296 | tf_op jit(solution)/shard_map/ppermute | solution.py:76
  19.4 87.6 %collective-permute-start.1 = (bf16[1,8,1,8,256]{4,3,2,1,0:T(8,128)(2,1)S(1)}, bf16[1,8,1,8,256]{4,3,2,1,0:T(8,128)(2,1)S(1)}, u32[]{:S(2)}, u32[]{:S(2)}) collective-permute-start(bf16[1,8,1,8,256]{4,3,2,1,0:T(8,128)(2,1)S(1)} %get-tuple-element.1494), channel_id=1, source_target_pairs={{1,0},{3,2},{5,4},{7,6},{9,8},{11,10},{13,12},{15,14},{17,16},{19,... | collective-permute-start | bytes 98312 | tf_op jit(solution)/shard_map/ppermute | solution.py:76
  96.8 10.2 %collective-permute-start = (bf16[1,8,1,8,256]{4,3,2,1,0:T(8,128)(2,1)S(1)}, bf16[1,8,1,8,256]{4,3,2,1,0:T(8,128)(2,1)S(1)}, u32[]{:S(2)}, u32[]{:S(2)}) collective-permute-start(bf16[1,8,1,8,256]{4,3,2,1,0:T(8,128)(2,1)S(1)} %get-tuple-element.1493), channel_id=1, source_target_pairs={{0,1},{2,3},{4,5},{6,7},{8,9},{10,11},{12,13},{14,15},{16,17},{18,... | collective-permute-start | bytes 98312 | tf_op jit(solution)/shard_map/ppermute | solution.py:76
  98.5 0.7 collective-permute-start.7
  99.2 7.5 %collective-permute-start.5 = (bf16[1,1,1,8,256]{4,3,2,1,0:T(8,128)(2,1)S(1)}, bf16[1,1,1,8,256]{4,3,2,1,0:T(8,128)(2,1)S(1)}, u32[]{:S(2)}, u32[]{:S(2)}) collective-permute-start(bf16[1,1,1,8,256]{4,3,2,1,0:T(8,128)(2,1)S(1)} %get-tuple-element.1487), channel_id=1, source_target_pairs={{0,3},{2,5},{4,7},{8,11},{10,13},{12,15},{16,19},{18,21},{20,23},{... | collective-permute-start | bytes 12296 | tf_op jit(solution)/shard_map/ppermute | solution.py:76
  111.5 12.6 %collective-permute-start.8 = (bf16[512,128]{1,0:T(8,128)(2,1)S(1)}, bf16[512,128]{1,0:T(8,128)(2,1)S(1)}, u32[]{:S(2)}, u32[]{:S(2)}) collective-permute-start(bf16[512,128]{1,0:T(8,128)(2,1)S(1)} %fusion.3), channel_id=1, source_target_pairs={{8,0},{16,8},{24,16},{9,1},{17,9},{25,17},{10,2},{18,10},{26,18},{... | collective-permute-start | bytes 393224 | tf_op jit(solution)/shard_map/ppermute | solution.py:160
  113.0 7.7 %collective-permute-start.13 = (bf16[1,1,1,8,128]{4,3,2,1,0:T(8,128)(2,1)S(1)}, bf16[1,1,1,8,128]{4,3,2,1,0:T(8,128)(2,1)S(1)}, u32[]{:S(2)}, u32[]{:S(2)}) collective-permute-start(bf16[1,1,1,8,128]{4,3,2,1,0:T(8,128)(2,1)S(1)} %get-tuple-element.1529), channel_id=1, source_target_pairs={{11,0},{13,2},{15,4},{19,8},{21,10},{23,12},{27,16},{29,18},{31,20}} | collective-permute-start | bytes 6152 | tf_op jit(solution)/shard_map/ppermute | solution.py:76
  114.3 9.5 %collective-permute-start.12 = (bf16[1,1,8,8,128]{4,3,2,1,0:T(8,128)(2,1)S(1)}, bf16[1,1,8,8,128]{4,3,2,1,0:T(8,128)(2,1)S(1)}, u32[]{:S(2)}, u32[]{:S(2)}) collective-permute-start(bf16[1,1,8,8,128]{4,3,2,1,0:T(8,128)(2,1)S(1)} %get-tuple-element.1532), channel_id=1, source_target_pairs={{10,0},{11,1},{12,2},{13,3},{14,4},{15,5},{18,8},{19,9},{20,10},{2... | collective-permute-start | bytes 49160 | tf_op jit(solution)/shard_map/ppermute | solution.py:76
  115.6 5.8 %collective-permute-start.11 = (bf16[1,1,1,8,128]{4,3,2,1,0:T(8,128)(2,1)S(1)}, bf16[1,1,1,8,128]{4,3,2,1,0:T(8,128)(2,1)S(1)}, u32[]{:S(2)}, u32[]{:S(2)}) collective-permute-start(bf16[1,1,1,8,128]{4,3,2,1,0:T(8,128)(2,1)S(1)} %get-tuple-element.1530), channel_id=1, source_target_pairs={{10,1},{12,3},{14,5},{18,9},{20,11},{22,13},{26,17},{28,19},{30,21}} | collective-permute-start | bytes 6152 | tf_op jit(solution)/shard_map/ppermute | solution.py:76
  116.3 7.6 %collective-permute-start.10 = (bf16[1,8,1,8,128]{4,3,2,1,0:T(8,128)(2,1)S(1)}, bf16[1,8,1,8,128]{4,3,2,1,0:T(8,128)(2,1)S(1)}, u32[]{:S(2)}, u32[]{:S(2)}) collective-permute-start(bf16[1,8,1,8,128]{4,3,2,1,0:T(8,128)(2,1)S(1)} %get-tuple-element.1534), channel_id=1, source_target_pairs={{9,0},{11,2},{13,4},{15,6},{17,8},{19,10},{21,12},{23,14},{25,16},... | collective-permute-start | bytes 49160 | tf_op jit(solution)/shard_map/ppermute | solution.py:76
  120.7 3.3 %collective-permute-start.9 = (bf16[1,8,1,8,128]{4,3,2,1,0:T(8,128)(2,1)S(1)}, bf16[1,8,1,8,128]{4,3,2,1,0:T(8,128)(2,1)S(1)}, u32[]{:S(2)}, u32[]{:S(2)}) collective-permute-start(bf16[1,8,1,8,128]{4,3,2,1,0:T(8,128)(2,1)S(1)} %get-tuple-element.1533), channel_id=1, source_target_pairs={{8,1},{10,3},{12,5},{14,7},{16,9},{18,11},{20,13},{22,15},{24,17},... | collective-permute-start | bytes 49160 | tf_op jit(solution)/shard_map/ppermute | solution.py:76
  122.1 0.7 collective-permute-start.14
  122.8 1.2 collective-permute-start.15
  128.5 24.9 %collective-permute-start.17 = (bf16[512,128]{1,0:T(8,128)(2,1)S(1)}, bf16[512,128]{1,0:T(8,128)(2,1)S(1)}, u32[]{:S(2)}, u32[]{:S(2)}) collective-permute-start(bf16[512,128]{1,0:T(8,128)(2,1)S(1)} %fusion.6), channel_id=1, source_target_pairs={{8,0},{16,8},{24,16},{9,1},{17,9},{25,17},{10,2},{18,10},{26,18},{... | collective-permute-start | bytes 393224 | tf_op jit(solution)/shard_map/ppermute | solution.py:160
  129.8 20.3 %collective-permute-start.22 = (bf16[1,1,1,8,128]{4,3,2,1,0:T(8,128)(2,1)S(1)}, bf16[1,1,1,8,128]{4,3,2,1,0:T(8,128)(2,1)S(1)}, u32[]{:S(2)}, u32[]{:S(2)}) collective-permute-start(bf16[1,1,1,8,128]{4,3,2,1,0:T(8,128)(2,1)S(1)} %get-tuple-element.1519), channel_id=1, source_target_pairs={{11,0},{13,2},{15,4},{19,8},{21,10},{23,12},{27,16},{29,18},{31,20}} | collective-permute-start | bytes 6152 | tf_op jit(solution)/shard_map/ppermute | solution.py:76
  131.1 22.0 %collective-permute-start.21 = (bf16[1,1,8,8,128]{4,3,2,1,0:T(8,128)(2,1)S(1)}, bf16[1,1,8,8,128]{4,3,2,1,0:T(8,128)(2,1)S(1)}, u32[]{:S(2)}, u32[]{:S(2)}) collective-permute-start(bf16[1,1,8,8,128]{4,3,2,1,0:T(8,128)(2,1)S(1)} %get-tuple-element.1522), channel_id=1, source_target_pairs={{10,0},{11,1},{12,2},{13,3},{14,4},{15,5},{18,8},{19,9},{20,10},{2... | collective-permute-start | bytes 49160 | tf_op jit(solution)/shard_map/ppermute | solution.py:76
  132.4 18.4 %collective-permute-start.20 = (bf16[1,1,1,8,128]{4,3,2,1,0:T(8,128)(2,1)S(1)}, bf16[1,1,1,8,128]{4,3,2,1,0:T(8,128)(2,1)S(1)}, u32[]{:S(2)}, u32[]{:S(2)}) collective-permute-start(bf16[1,1,1,8,128]{4,3,2,1,0:T(8,128)(2,1)S(1)} %get-tuple-element.1520), channel_id=1, source_target_pairs={{10,1},{12,3},{14,5},{18,9},{20,11},{22,13},{26,17},{28,19},{30,21}} | collective-permute-start | bytes 6152 | tf_op jit(solution)/shard_map/ppermute | solution.py:76
  133.1 20.1 %collective-permute-start.19 = (bf16[1,8,1,8,128]{4,3,2,1,0:T(8,128)(2,1)S(1)}, bf16[1,8,1,8,128]{4,3,2,1,0:T(8,128)(2,1)S(1)}, u32[]{:S(2)}, u32[]{:S(2)}) collective-permute-start(bf16[1,8,1,8,128]{4,3,2,1,0:T(8,128)(2,1)S(1)} %get-tuple-element.1524), channel_id=1, source_target_pairs={{9,0},{11,2},{13,4},{15,6},{17,8},{19,10},{21,12},{23,14},{25,16},... | collective-permute-start | bytes 49160 | tf_op jit(solution)/shard_map/ppermute | solution.py:76
  150.1 3.1 %collective-permute-start.18 = (bf16[1,8,1,8,128]{4,3,2,1,0:T(8,128)(2,1)S(1)}, bf16[1,8,1,8,128]{4,3,2,1,0:T(8,128)(2,1)S(1)}, u32[]{:S(2)}, u32[]{:S(2)}) collective-permute-start(bf16[1,8,1,8,128]{4,3,2,1,0:T(8,128)(2,1)S(1)} %get-tuple-element.1523), channel_id=1, source_target_pairs={{8,1},{10,3},{12,5},{14,7},{16,9},{18,11},{20,13},{22,15},{24,17},... | collective-permute-start | bytes 49160 | tf_op jit(solution)/shard_map/ppermute | solution.py:76
  152.3 1.0 collective-permute-start.24
  157.7 28.8 %collective-permute-start.26 = (bf16[512,128]{1,0:T(8,128)(2,1)S(1)}, bf16[512,128]{1,0:T(8,128)(2,1)S(1)}, u32[]{:S(2)}, u32[]{:S(2)}) collective-permute-start(bf16[512,128]{1,0:T(8,128)(2,1)S(1)} %fusion.9), channel_id=1, source_target_pairs={{8,0},{16,8},{24,16},{9,1},{17,9},{25,17},{10,2},{18,10},{26,18},{... | collective-permute-start | bytes 393224 | tf_op jit(solution)/shard_map/ppermute | solution.py:160
  159.1 24.0 %collective-permute-start.31 = (bf16[1,1,1,8,128]{4,3,2,1,0:T(8,128)(2,1)S(1)}, bf16[1,1,1,8,128]{4,3,2,1,0:T(8,128)(2,1)S(1)}, u32[]{:S(2)}, u32[]{:S(2)}) collective-permute-start(bf16[1,1,1,8,128]{4,3,2,1,0:T(8,128)(2,1)S(1)} %get-tuple-element.1509), channel_id=1, source_target_pairs={{11,0},{13,2},{15,4},{19,8},{21,10},{23,12},{27,16},{29,18},{31,20}} | collective-permute-start | bytes 6152 | tf_op jit(solution)/shard_map/ppermute | solution.py:76
  160.4 25.8 %collective-permute-start.30 = (bf16[1,1,8,8,128]{4,3,2,1,0:T(8,128)(2,1)S(1)}, bf16[1,1,8,8,128]{4,3,2,1,0:T(8,128)(2,1)S(1)}, u32[]{:S(2)}, u32[]{:S(2)}) collective-permute-start(bf16[1,1,8,8,128]{4,3,2,1,0:T(8,128)(2,1)S(1)} %get-tuple-element.1512), channel_id=1, source_target_pairs={{10,0},{11,1},{12,2},{13,3},{14,4},{15,5},{18,8},{19,9},{20,10},{2... | collective-permute-start | bytes 49160 | tf_op jit(solution)/shard_map/ppermute | solution.py:76
  161.7 22.0 %collective-permute-start.29 = (bf16[1,1,1,8,128]{4,3,2,1,0:T(8,128)(2,1)S(1)}, bf16[1,1,1,8,128]{4,3,2,1,0:T(8,128)(2,1)S(1)}, u32[]{:S(2)}, u32[]{:S(2)}) collective-permute-start(bf16[1,1,1,8,128]{4,3,2,1,0:T(8,128)(2,1)S(1)} %get-tuple-element.1510), channel_id=1, source_target_pairs={{10,1},{12,3},{14,5},{18,9},{20,11},{22,13},{26,17},{28,19},{30,21}} | collective-permute-start | bytes 6152 | tf_op jit(solution)/shard_map/ppermute | solution.py:76
  162.4 23.9 %collective-permute-start.28 = (bf16[1,8,1,8,128]{4,3,2,1,0:T(8,128)(2,1)S(1)}, bf16[1,8,1,8,128]{4,3,2,1,0:T(8,128)(2,1)S(1)}, u32[]{:S(2)}, u32[]{:S(2)}) collective-permute-start(bf16[1,8,1,8,128]{4,3,2,1,0:T(8,128)(2,1)S(1)} %get-tuple-element.1514), channel_id=1, source_target_pairs={{9,0},{11,2},{13,4},{15,6},{17,8},{19,10},{21,12},{23,14},{25,16},... | collective-permute-start | bytes 49160 | tf_op jit(solution)/shard_map/ppermute | solution.py:76
  183.0 3.3 %collective-permute-start.27 = (bf16[1,8,1,8,128]{4,3,2,1,0:T(8,128)(2,1)S(1)}, bf16[1,8,1,8,128]{4,3,2,1,0:T(8,128)(2,1)S(1)}, u32[]{:S(2)}, u32[]{:S(2)}) collective-permute-start(bf16[1,8,1,8,128]{4,3,2,1,0:T(8,128)(2,1)S(1)} %get-tuple-element.1513), channel_id=1, source_target_pairs={{8,1},{10,3},{12,5},{14,7},{16,9},{18,11},{20,13},{22,15},{24,17},... | collective-permute-start | bytes 49160 | tf_op jit(solution)/shard_map/ppermute | solution.py:76
  185.2 1.2 collective-permute-start.33
  204.7 64.1 %all-reduce.47.cloned.1.call-start = ((), (), s32[]{:S(2)}) async-start(), calls=%async_computation.2 | async-start | bytes 442368 | tf_op jit(solution)/shard_map/psum | solution.py:170
  (8 other events, 9.0 us)
Sparse Core Ops, SparseCore 0:
  204.8 43.4 reduce-scatter.1
  250.7 18.0 all-reduce.46
where the time goes:
time: 279 us; the launch traced here: 277 us
  waiting for transfers between devices  92 us (33%)
  between operations  68 us (24%)
  starting transfers between devices  43.7 us (16%)
  local copies, waits for them, and re-layouts  31.8 us (11%)
  blocking collectives  19.6 us (7%)
  other arithmetic  13.3 us (5%)
  matrix products  8.99 us (3%)
    ppermute x32, starting transfers between devices, exchange(): received[shift_x, shift_y] = lax.ppermute(piece, axes, route)  39.7 us
    ppermute x32, waiting for transfers between devices, exchange(): received[shift_x, shift_y] = lax.ppermute(piece, axes, route)  36.5 us
    reduce_scatter x1, waiting for transfers between devices, shards(): lax.psum_scatter(lax.slice_in_dim(summed, 0, shard_rows * n_x, axis=0).as...  36.1 us
    unnamed x126, local copies, waits for them, and re-layouts  22.9 us
    all_gather x1, blocking collectives, shards(): weights = lax.all_gather(kernel[0], 'sx', axis=0, tiled=True)  19.6 us
    psum x1, waiting for transfers between devices, shards(): lax.psum(kernel_term.astype(jnp.bfloat16), 'sy').astype(jnp.float32)  19.4 us
    dot_general x4, matrix products, shards(): jnp.dot(columns(grad_pad, row_count, -1), flipped, preferred_element_type...  6.82 us
  transfers between devices with their start and end apart: 37, of which 5 were waited for; matrix products, arithmetic and copies ran while one was open for 7% of the time, Pallas kernels for 0%

commit v1 on v0

--- a/solution.py
+++ b/solution.py
@@ -167,7 +167,9 @@
     norm_scale = float(n_x * n_y * micro_count * row_count) ** (-0.5)
     kernel_term = kernel_total * norm_scale
     shard_rows = kernel.shape[1]
-    summed = lax.psum(kernel_term.astype(jnp.bfloat16), "sy").astype(jnp.float32)
+    summed = jnp.sum(lax.all_gather(kernel_term.astype(jnp.bfloat16), "sy"), axis=0).astype(
+        jnp.float32
+    )
     kernel_share = lax.psum_scatter(
         lax.slice_in_dim(summed, 0, shard_rows * n_x, axis=0).astype(jnp.bfloat16),
         "sx",

time: 279 us -> 269 us (0.964)
  waiting for transfers between devices: 92 us -> 78.5 us
  other arithmetic: 13.3 us -> 16.2 us
    all_gather x0 -> x1, waiting for transfers between devices: none -> 21 us  [shards(): lax.all_gather(kernel_term.astype(jnp.bfloat16), 'sy')]
    psum x1 -> x0, waiting for transfers between devices: 19.4 us -> none  [shards(): lax.psum(kernel_term.astype(jnp.bfloat16), 'sy').astype(jnp.float32)]
    reduce_scatter x1, waiting for transfers between devices: 36.1 us -> 21 us  [shards(): lax.psum_scatter(lax.slice_in_dim(summed, 0, shard_rows * n_x, axis=0).as...]
    reduce_sum x0 -> x1, other arithmetic: none -> 2.97 us  [shards(): jnp.sum(lax.all_gather(kernel_term.astype(jnp.bfloat16), 'sy'), axis=0)]
  transfers between devices with their start and end apart: 37 -> 37, of which waited for: 5 -> 5; matrix products, arithmetic and copies ran while one was open for 7% -> 9% of each run, Pallas kernels for 0% -> 0%
where the time goes in v1:
time: 269 us; the launch traced here: 267 us
  waiting for transfers between devices  78.5 us (29%)
  between operations  68 us (25%)
  starting transfers between devices  43.7 us (16%)
  local copies, waits for them, and re-layouts  31.8 us (12%)
  blocking collectives  19.6 us (7%)
  other arithmetic  16.2 us (6%)
  matrix products  8.98 us (3%)
    ppermute x32, starting transfers between devices, exchange(): received[shift_x, shift_y] = lax.ppermute(piece, axes, route)  39.7 us
    ppermute x32, waiting for transfers between devices, exchange(): received[shift_x, shift_y] = lax.ppermute(piece, axes, route)  36.5 us
    unnamed x126, local copies, waits for them, and re-layouts  22.9 us
    all_gather x1, waiting for transfers between devices, shards(): lax.all_gather(kernel_term.astype(jnp.bfloat16), 'sy')  21 us
    reduce_scatter x1, waiting for transfers between devices, shards(): lax.psum_scatter(lax.slice_in_dim(summed, 0, shard_rows * n_x, axis=0).as...  21 us
    all_gather x1, blocking collectives, shards(): weights = lax.all_gather(kernel[0], 'sx', axis=0, tiled=True)  19.6 us
    dot_general x4, matrix products, shards(): jnp.dot(columns(grad_pad, row_count, -1), flipped, preferred_element_type...  6.83 us
  transfers between devices with their start and end apart: 37, of which 5 were waited for; matrix products, arithmetic and copies ran while one was open for 9% of the time, Pallas kernels for 0%

profile of v1, /device:TPU:0, one launch (start us, length us, event | category | flops | bytes accessed | tf_op | source)
XLA Modules:
  0.0 266.8 jit_solution(5664243946565253871)
XLA Ops:
  11.2 1.3 collective-permute-start.4
  12.5 4.8 %collective-permute-start.6 = (bf16[1,1,8,8,256]{4,3,2,1,0:T(8,128)(2,1)S(1)}, bf16[1,1,8,8,256]{4,3,2,1,0:T(8,128)(2,1)S(1)}, u32[]{:S(2)}, u32[]{:S(2)}) collective-permute-start(bf16[1,1,8,8,256]{4,3,2,1,0:T(8,128)(2,1)S(1)} %get-tuple-element.1491), channel_id=1, source_target_pairs={{0,2},{1,3},{2,4},{3,5},{4,6},{5,7},{8,10},{9,11},{10,12},{11,13},... | collective-permute-start | bytes 98312 | tf_op jit(solution)/shard_map/ppermute | solution.py:76
  17.4 1.3 collective-permute-start.3
  19.4 1.3 collective-permute-start.1
  20.7 2.1 fusion.89
  36.6 1.6 fusion.90
  46.1 19.6 %all-gather = bf16[1,3456,128]{2,1,0:T(8,128)(2,1)S(1)} all-gather(bf16[1,864,128]{2,1,0:T(8,128)(2,1)} %param.11), channel_id=2, replica_groups=mesh['pipe'=4,'sx'=4,'sy'=2] {'sx'}, dimensions={1}, use_global_device_ids=true | all-gather | bytes 1105920 | tf_op jit(solution)/shard_map/all_gather | solution.py:116
  80.3 1.3 copy.138
  96.8 1.6 collective-permute-start
  99.2 6.2 %collective-permute-start.5 = (bf16[1,1,1,8,256]{4,3,2,1,0:T(8,128)(2,1)S(1)}, bf16[1,1,1,8,256]{4,3,2,1,0:T(8,128)(2,1)S(1)}, u32[]{:S(2)}, u32[]{:S(2)}) collective-permute-start(bf16[1,1,1,8,256]{4,3,2,1,0:T(8,128)(2,1)S(1)} %get-tuple-element.1487), channel_id=1, source_target_pairs={{0,3},{2,5},{4,7},{8,11},{10,13},{12,15},{16,19},{18,21},{20,23},{... | collective-permute-start | bytes 12296 | tf_op jit(solution)/shard_map/ppermute | solution.py:76
  105.4 1.3 collective-permute-done.5
  110.0 1.2 fusion.35
  111.5 1.3 collective-permute-start.8
  113.0 1.3 collective-permute-start.13
  114.3 1.3 collective-permute-start.12
  116.3 1.3 collective-permute-start.10
  128.5 1.3 collective-permute-start.17
  129.8 1.3 collective-permute-start.22
  131.1 1.3 collective-permute-start.21
  133.1 1.3 collective-permute-start.19
  134.4 15.8 %collective-permute-done.22 = bf16[1,1,1,8,128]{4,3,2,1,0:T(8,128)(2,1)S(1)} collective-permute-done((bf16[1,1,1,8,128]{4,3,2,1,0:T(8,128)(2,1)S(1)}, bf16[1,1,1,8,128]{4,3,2,1,0:T(8,128)(2,1)S(1)}, u32[]{:S(2)}, u32[]{:S(2)}) %collective-permute-start.22) | collective-permute-done | bytes 2080 | tf_op jit(solution)/shard_map/ppermute | solution.py:76
  157.8 1.3 collective-permute-start.26
  159.1 1.3 collective-permute-start.31
  160.4 1.3 collective-permute-start.30
  162.4 1.3 collective-permute-start.28
  163.7 19.4 %collective-permute-done.31 = bf16[1,1,1,8,128]{4,3,2,1,0:T(8,128)(2,1)S(1)} collective-permute-done((bf16[1,1,1,8,128]{4,3,2,1,0:T(8,128)(2,1)S(1)}, bf16[1,1,1,8,128]{4,3,2,1,0:T(8,128)(2,1)S(1)}, u32[]{:S(2)}, u32[]{:S(2)}) %collective-permute-start.31) | collective-permute-done | bytes 2080 | tf_op jit(solution)/shard_map/ppermute | solution.py:76
  198.0 2.1 fusion
  206.2 21.0 %all-gather.4.cloned.1.call-done = bf16[6912,128]{1,0:T(8,128)(2,1)} async-done(((bf16[3456,128]{1,0:T(8,128)(2,1)}), bf16[6912,128]{1,0:T(8,128)(2,1)}) %all-gather.4.cloned.1.call-update) | async-done | bytes 1769488 | tf_op jit(solution)/shard_map/all_gather | solution.py:170
  227.2 3.0 %reduce_sum.65 = bf16[3456,128]{1,0:T(8,128)(2,1)} reduce(bf16[2,3456,128]{2,1,0:T(8,128)(2,1)} %bitcast.948, bf16[]{:T(256)} %constant.59.clone.1), dimensions={0}, to_apply=%region_5.6 | reduce | flops 442368 | bytes 2654210 | tf_op jit(solution)/shard_map/reduce_sum | solution.py:170
  233.1 3.2 %fusion.38 = (f32[512]{0:T(512)S(1)}, f32[512,128]{1,0:T(8,128)S(1)}) fusion(bf16[1,1,1,1,512,128]{5,4,3,2,1,0:T(8,128)(2,1)S(1)} %copy-done, f32[128]{0:T(128)S(1)} %bitcast.972, f32[512]{0:T(512)S(1)} %fusion.70, bf16[512,3456]{1,0:T(8,128)(2,1)} %bitcast.281, bf16[3456,128]{1,0:T(8,128)(2,1)S(1)} %bitcast.952), kind=kOutput, calls=%fused_computation.238 | convolution fusion | flops 453967360 | bytes 4821504 | tf_op jit(solution)/shard_map/dot_general | solution.py:152
  237.3 21.0 %reduce-scatter.2.cloned.1.call-done = bf16[864,128]{1,0:T(8,128)(2,1)} async-done(((bf16[3456,128]{1,0:T(8,128)(2,1)}), bf16[864,128]{1,0:T(8,128)(2,1)}) %reduce-scatter.2.cloned.1.call-update) | async-done | bytes 221200 | tf_op jit(solution)/shard_map/reduce_scatter | solution.py:173
  258.2 1.7 bitcast_convert_fusion
  (347 shorter events, 52.6 us)
Async XLA Ops:
  7.2 220.1 %all-gather.4.cloned.1.call-start = ((), (), s32[]{:S(2)}) async-start(), calls=%async_computation.2 | async-start | bytes 2654208 | tf_op jit(solution)/shard_map/all_gather | solution.py:170
  11.2 85.6 %collective-permute-start.4 = (bf16[1,1,1,8,256]{4,3,2,1,0:T(8,128)(2,1)S(1)}, bf16[1,1,1,8,256]{4,3,2,1,0:T(8,128)(2,1)S(1)}, u32[]{:S(2)}, u32[]{:S(2)}) collective-permute-start(bf16[1,1,1,8,256]{4,3,2,1,0:T(8,128)(2,1)S(1)} %get-tuple-element.1489), channel_id=1, source_target_pairs={{3,0},{5,2},{7,4},{11,8},{13,10},{15,12},{19,16},{21,18},{23,20},{... | collective-permute-start | bytes 12296 | tf_op jit(solution)/shard_map/ppermute | solution.py:76
  12.5 94.6 %collective-permute-start.6 = (bf16[1,1,8,8,256]{4,3,2,1,0:T(8,128)(2,1)S(1)}, bf16[1,1,8,8,256]{4,3,2,1,0:T(8,128)(2,1)S(1)}, u32[]{:S(2)}, u32[]{:S(2)}) collective-permute-start(bf16[1,1,8,8,256]{4,3,2,1,0:T(8,128)(2,1)S(1)} %get-tuple-element.1491), channel_id=1, source_target_pairs={{0,2},{1,3},{2,4},{3,5},{4,6},{5,7},{8,10},{9,11},{10,12},{11,13},... | collective-permute-start | bytes 98312 | tf_op jit(solution)/shard_map/ppermute | solution.py:76
  17.4 89.5 %collective-permute-start.3 = (bf16[1,1,8,8,256]{4,3,2,1,0:T(8,128)(2,1)S(1)}, bf16[1,1,8,8,256]{4,3,2,1,0:T(8,128)(2,1)S(1)}, u32[]{:S(2)}, u32[]{:S(2)}) collective-permute-start(bf16[1,1,8,8,256]{4,3,2,1,0:T(8,128)(2,1)S(1)} %get-tuple-element.1492), channel_id=1, source_target_pairs={{2,0},{3,1},{4,2},{5,3},{6,4},{7,5},{10,8},{11,9},{12,10},{13,11},... | collective-permute-start | bytes 98312 | tf_op jit(solution)/shard_map/ppermute | solution.py:76
  18.7 79.8 %collective-permute-start.2 = (bf16[1,1,1,8,256]{4,3,2,1,0:T(8,128)(2,1)S(1)}, bf16[1,1,1,8,256]{4,3,2,1,0:T(8,128)(2,1)S(1)}, u32[]{:S(2)}, u32[]{:S(2)}) collective-permute-start(bf16[1,1,1,8,256]{4,3,2,1,0:T(8,128)(2,1)S(1)} %get-tuple-element.1488), channel_id=1, source_target_pairs={{2,1},{4,3},{6,5},{10,9},{12,11},{14,13},{18,17},{20,19},{22,21},{... | collective-permute-start | bytes 12296 | tf_op jit(solution)/shard_map/ppermute | solution.py:76
  19.4 87.6 %collective-permute-start.1 = (bf16[1,8,1,8,256]{4,3,2,1,0:T(8,128)(2,1)S(1)}, bf16[1,8,1,8,256]{4,3,2,1,0:T(8,128)(2,1)S(1)}, u32[]{:S(2)}, u32[]{:S(2)}) collective-permute-start(bf16[1,8,1,8,256]{4,3,2,1,0:T(8,128)(2,1)S(1)} %get-tuple-element.1494), channel_id=1, source_target_pairs={{1,0},{3,2},{5,4},{7,6},{9,8},{11,10},{13,12},{15,14},{17,16},{19,... | collective-permute-start | bytes 98312 | tf_op jit(solution)/shard_map/ppermute | solution.py:76
  96.8 10.2 %collective-permute-start = (bf16[1,8,1,8,256]{4,3,2,1,0:T(8,128)(2,1)S(1)}, bf16[1,8,1,8,256]{4,3,2,1,0:T(8,128)(2,1)S(1)}, u32[]{:S(2)}, u32[]{:S(2)}) collective-permute-start(bf16[1,8,1,8,256]{4,3,2,1,0:T(8,128)(2,1)S(1)} %get-tuple-element.1493), channel_id=1, source_target_pairs={{0,1},{2,3},{4,5},{6,7},{8,9},{10,11},{12,13},{14,15},{16,17},{18,... | collective-permute-start | bytes 98312 | tf_op jit(solution)/shard_map/ppermute | solution.py:76
  98.5 0.7 collective-permute-start.7
  99.2 7.5 %collective-permute-start.5 = (bf16[1,1,1,8,256]{4,3,2,1,0:T(8,128)(2,1)S(1)}, bf16[1,1,1,8,256]{4,3,2,1,0:T(8,128)(2,1)S(1)}, u32[]{:S(2)}, u32[]{:S(2)}) collective-permute-start(bf16[1,1,1,8,256]{4,3,2,1,0:T(8,128)(2,1)S(1)} %get-tuple-element.1487), channel_id=1, source_target_pairs={{0,3},{2,5},{4,7},{8,11},{10,13},{12,15},{16,19},{18,21},{20,23},{... | collective-permute-start | bytes 12296 | tf_op jit(solution)/shard_map/ppermute | solution.py:76
  111.5 12.6 %collective-permute-start.8 = (bf16[512,128]{1,0:T(8,128)(2,1)S(1)}, bf16[512,128]{1,0:T(8,128)(2,1)S(1)}, u32[]{:S(2)}, u32[]{:S(2)}) collective-permute-start(bf16[512,128]{1,0:T(8,128)(2,1)S(1)} %fusion.3), channel_id=1, source_target_pairs={{8,0},{16,8},{24,16},{9,1},{17,9},{25,17},{10,2},{18,10},{26,18},{... | collective-permute-start | bytes 393224 | tf_op jit(solution)/shard_map/ppermute | solution.py:160
  113.0 7.7 %collective-permute-start.13 = (bf16[1,1,1,8,128]{4,3,2,1,0:T(8,128)(2,1)S(1)}, bf16[1,1,1,8,128]{4,3,2,1,0:T(8,128)(2,1)S(1)}, u32[]{:S(2)}, u32[]{:S(2)}) collective-permute-start(bf16[1,1,1,8,128]{4,3,2,1,0:T(8,128)(2,1)S(1)} %get-tuple-element.1529), channel_id=1, source_target_pairs={{11,0},{13,2},{15,4},{19,8},{21,10},{23,12},{27,16},{29,18},{31,20}} | collective-permute-start | bytes 6152 | tf_op jit(solution)/shard_map/ppermute | solution.py:76
  114.3 9.5 %collective-permute-start.12 = (bf16[1,1,8,8,128]{4,3,2,1,0:T(8,128)(2,1)S(1)}, bf16[1,1,8,8,128]{4,3,2,1,0:T(8,128)(2,1)S(1)}, u32[]{:S(2)}, u32[]{:S(2)}) collective-permute-start(bf16[1,1,8,8,128]{4,3,2,1,0:T(8,128)(2,1)S(1)} %get-tuple-element.1532), channel_id=1, source_target_pairs={{10,0},{11,1},{12,2},{13,3},{14,4},{15,5},{18,8},{19,9},{20,10},{2... | collective-permute-start | bytes 49160 | tf_op jit(solution)/shard_map/ppermute | solution.py:76
  115.6 5.8 %collective-permute-start.11 = (bf16[1,1,1,8,128]{4,3,2,1,0:T(8,128)(2,1)S(1)}, bf16[1,1,1,8,128]{4,3,2,1,0:T(8,128)(2,1)S(1)}, u32[]{:S(2)}, u32[]{:S(2)}) collective-permute-start(bf16[1,1,1,8,128]{4,3,2,1,0:T(8,128)(2,1)S(1)} %get-tuple-element.1530), channel_id=1, source_target_pairs={{10,1},{12,3},{14,5},{18,9},{20,11},{22,13},{26,17},{28,19},{30,21}} | collective-permute-start | bytes 6152 | tf_op jit(solution)/shard_map/ppermute | solution.py:76
  116.3 7.6 %collective-permute-start.10 = (bf16[1,8,1,8,128]{4,3,2,1,0:T(8,128)(2,1)S(1)}, bf16[1,8,1,8,128]{4,3,2,1,0:T(8,128)(2,1)S(1)}, u32[]{:S(2)}, u32[]{:S(2)}) collective-permute-start(bf16[1,8,1,8,128]{4,3,2,1,0:T(8,128)(2,1)S(1)} %get-tuple-element.1534), channel_id=1, source_target_pairs={{9,0},{11,2},{13,4},{15,6},{17,8},{19,10},{21,12},{23,14},{25,16},... | collective-permute-start | bytes 49160 | tf_op jit(solution)/shard_map/ppermute | solution.py:76
  120.7 3.3 %collective-permute-start.9 = (bf16[1,8,1,8,128]{4,3,2,1,0:T(8,128)(2,1)S(1)}, bf16[1,8,1,8,128]{4,3,2,1,0:T(8,128)(2,1)S(1)}, u32[]{:S(2)}, u32[]{:S(2)}) collective-permute-start(bf16[1,8,1,8,128]{4,3,2,1,0:T(8,128)(2,1)S(1)} %get-tuple-element.1533), channel_id=1, source_target_pairs={{8,1},{10,3},{12,5},{14,7},{16,9},{18,11},{20,13},{22,15},{24,17},... | collective-permute-start | bytes 49160 | tf_op jit(solution)/shard_map/ppermute | solution.py:76
  121.4 0.7 collective-permute-start.16
  122.8 1.2 collective-permute-start.15
  128.5 24.9 %collective-permute-start.17 = (bf16[512,128]{1,0:T(8,128)(2,1)S(1)}, bf16[512,128]{1,0:T(8,128)(2,1)S(1)}, u32[]{:S(2)}, u32[]{:S(2)}) collective-permute-start(bf16[512,128]{1,0:T(8,128)(2,1)S(1)} %fusion.6), channel_id=1, source_target_pairs={{8,0},{16,8},{24,16},{9,1},{17,9},{25,17},{10,2},{18,10},{26,18},{... | collective-permute-start | bytes 393224 | tf_op jit(solution)/shard_map/ppermute | solution.py:160
  129.8 20.3 %collective-permute-start.22 = (bf16[1,1,1,8,128]{4,3,2,1,0:T(8,128)(2,1)S(1)}, bf16[1,1,1,8,128]{4,3,2,1,0:T(8,128)(2,1)S(1)}, u32[]{:S(2)}, u32[]{:S(2)}) collective-permute-start(bf16[1,1,1,8,128]{4,3,2,1,0:T(8,128)(2,1)S(1)} %get-tuple-element.1519), channel_id=1, source_target_pairs={{11,0},{13,2},{15,4},{19,8},{21,10},{23,12},{27,16},{29,18},{31,20}} | collective-permute-start | bytes 6152 | tf_op jit(solution)/shard_map/ppermute | solution.py:76
  131.1 22.0 %collective-permute-start.21 = (bf16[1,1,8,8,128]{4,3,2,1,0:T(8,128)(2,1)S(1)}, bf16[1,1,8,8,128]{4,3,2,1,0:T(8,128)(2,1)S(1)}, u32[]{:S(2)}, u32[]{:S(2)}) collective-permute-start(bf16[1,1,8,8,128]{4,3,2,1,0:T(8,128)(2,1)S(1)} %get-tuple-element.1522), channel_id=1, source_target_pairs={{10,0},{11,1},{12,2},{13,3},{14,4},{15,5},{18,8},{19,9},{20,10},{2... | collective-permute-start | bytes 49160 | tf_op jit(solution)/shard_map/ppermute | solution.py:76
  132.4 18.4 %collective-permute-start.20 = (bf16[1,1,1,8,128]{4,3,2,1,0:T(8,128)(2,1)S(1)}, bf16[1,1,1,8,128]{4,3,2,1,0:T(8,128)(2,1)S(1)}, u32[]{:S(2)}, u32[]{:S(2)}) collective-permute-start(bf16[1,1,1,8,128]{4,3,2,1,0:T(8,128)(2,1)S(1)} %get-tuple-element.1520), channel_id=1, source_target_pairs={{10,1},{12,3},{14,5},{18,9},{20,11},{22,13},{26,17},{28,19},{30,21}} | collective-permute-start | bytes 6152 | tf_op jit(solution)/shard_map/ppermute | solution.py:76
  133.1 20.1 %collective-permute-start.19 = (bf16[1,8,1,8,128]{4,3,2,1,0:T(8,128)(2,1)S(1)}, bf16[1,8,1,8,128]{4,3,2,1,0:T(8,128)(2,1)S(1)}, u32[]{:S(2)}, u32[]{:S(2)}) collective-permute-start(bf16[1,8,1,8,128]{4,3,2,1,0:T(8,128)(2,1)S(1)} %get-tuple-element.1524), channel_id=1, source_target_pairs={{9,0},{11,2},{13,4},{15,6},{17,8},{19,10},{21,12},{23,14},{25,16},... | collective-permute-start | bytes 49160 | tf_op jit(solution)/shard_map/ppermute | solution.py:76
  150.1 3.1 %collective-permute-start.18 = (bf16[1,8,1,8,128]{4,3,2,1,0:T(8,128)(2,1)S(1)}, bf16[1,8,1,8,128]{4,3,2,1,0:T(8,128)(2,1)S(1)}, u32[]{:S(2)}, u32[]{:S(2)}) collective-permute-start(bf16[1,8,1,8,128]{4,3,2,1,0:T(8,128)(2,1)S(1)} %get-tuple-element.1523), channel_id=1, source_target_pairs={{8,1},{10,3},{12,5},{14,7},{16,9},{18,11},{20,13},{22,15},{24,17},... | collective-permute-start | bytes 49160 | tf_op jit(solution)/shard_map/ppermute | solution.py:76
  152.3 1.0 collective-permute-start.24
  157.8 28.8 %collective-permute-start.26 = (bf16[512,128]{1,0:T(8,128)(2,1)S(1)}, bf16[512,128]{1,0:T(8,128)(2,1)S(1)}, u32[]{:S(2)}, u32[]{:S(2)}) collective-permute-start(bf16[512,128]{1,0:T(8,128)(2,1)S(1)} %fusion.9), channel_id=1, source_target_pairs={{8,0},{16,8},{24,16},{9,1},{17,9},{25,17},{10,2},{18,10},{26,18},{... | collective-permute-start | bytes 393224 | tf_op jit(solution)/shard_map/ppermute | solution.py:160
  159.1 24.0 %collective-permute-start.31 = (bf16[1,1,1,8,128]{4,3,2,1,0:T(8,128)(2,1)S(1)}, bf16[1,1,1,8,128]{4,3,2,1,0:T(8,128)(2,1)S(1)}, u32[]{:S(2)}, u32[]{:S(2)}) collective-permute-start(bf16[1,1,1,8,128]{4,3,2,1,0:T(8,128)(2,1)S(1)} %get-tuple-element.1509), channel_id=1, source_target_pairs={{11,0},{13,2},{15,4},{19,8},{21,10},{23,12},{27,16},{29,18},{31,20}} | collective-permute-start | bytes 6152 | tf_op jit(solution)/shard_map/ppermute | solution.py:76
  160.4 25.8 %collective-permute-start.30 = (bf16[1,1,8,8,128]{4,3,2,1,0:T(8,128)(2,1)S(1)}, bf16[1,1,8,8,128]{4,3,2,1,0:T(8,128)(2,1)S(1)}, u32[]{:S(2)}, u32[]{:S(2)}) collective-permute-start(bf16[1,1,8,8,128]{4,3,2,1,0:T(8,128)(2,1)S(1)} %get-tuple-element.1512), channel_id=1, source_target_pairs={{10,0},{11,1},{12,2},{13,3},{14,4},{15,5},{18,8},{19,9},{20,10},{2... | collective-permute-start | bytes 49160 | tf_op jit(solution)/shard_map/ppermute | solution.py:76
  161.7 22.0 %collective-permute-start.29 = (bf16[1,1,1,8,128]{4,3,2,1,0:T(8,128)(2,1)S(1)}, bf16[1,1,1,8,128]{4,3,2,1,0:T(8,128)(2,1)S(1)}, u32[]{:S(2)}, u32[]{:S(2)}) collective-permute-start(bf16[1,1,1,8,128]{4,3,2,1,0:T(8,128)(2,1)S(1)} %get-tuple-element.1510), channel_id=1, source_target_pairs={{10,1},{12,3},{14,5},{18,9},{20,11},{22,13},{26,17},{28,19},{30,21}} | collective-permute-start | bytes 6152 | tf_op jit(solution)/shard_map/ppermute | solution.py:76
  162.4 23.9 %collective-permute-start.28 = (bf16[1,8,1,8,128]{4,3,2,1,0:T(8,128)(2,1)S(1)}, bf16[1,8,1,8,128]{4,3,2,1,0:T(8,128)(2,1)S(1)}, u32[]{:S(2)}, u32[]{:S(2)}) collective-permute-start(bf16[1,8,1,8,128]{4,3,2,1,0:T(8,128)(2,1)S(1)} %get-tuple-element.1514), channel_id=1, source_target_pairs={{9,0},{11,2},{13,4},{15,6},{17,8},{19,10},{21,12},{23,14},{25,16},... | collective-permute-start | bytes 49160 | tf_op jit(solution)/shard_map/ppermute | solution.py:76
  183.0 3.3 %collective-permute-start.27 = (bf16[1,8,1,8,128]{4,3,2,1,0:T(8,128)(2,1)S(1)}, bf16[1,8,1,8,128]{4,3,2,1,0:T(8,128)(2,1)S(1)}, u32[]{:S(2)}, u32[]{:S(2)}) collective-permute-start(bf16[1,8,1,8,128]{4,3,2,1,0:T(8,128)(2,1)S(1)} %get-tuple-element.1513), channel_id=1, source_target_pairs={{8,1},{10,3},{12,5},{14,7},{16,9},{18,11},{20,13},{22,15},{24,17},... | collective-permute-start | bytes 49160 | tf_op jit(solution)/shard_map/ppermute | solution.py:76
  185.2 1.2 collective-permute-start.33
  200.2 58.1 %reduce-scatter.2.cloned.1.call-start = ((), (), s32[]{:S(2)}) async-start(), calls=%async_computation.1 | async-start | bytes 1105920 | tf_op jit(solution)/shard_map/reduce_scatter | solution.py:173
  (8 other events, 9.0 us)
Sparse Core Ops, SparseCore 0:
  200.3 26.8 all-gather.3
  230.3 27.8 reduce-scatter.1
